TPU v7x, 32 devices: a whole 2x2x4 slice. The times are simulated.
32 devices in a mesh: groups: 2 (over y), rows: 4 (over x, core), rep: 4 (over z).
Axes of the slice: x: 2, y: 2, z: 4, core: 2. Of those that a mesh axis runs over, the one named last changes fastest.
Arguments:
- images: bfloat16 [8, 64, 128, 256], P(('groups', 'rep'), 'rows'), parts along dimension 0, may hold values from -6 to 6
- cotangent: bfloat16 [8, 64, 128, 256], P(('groups', 'rep'), 'rows'), parts along dimension 0, may hold values from -6 to 6
- row_taps: float32 [102, 256], P('groups'), parts along dimension 0, may hold values from -0.875 to 0.875
- col_taps: float32 [102, 256], P('groups'), parts along dimension 0, may hold values from -0.875 to 0.875
- norm_gain: float32 [512], P('groups'), parts along dimension 0, may hold values from 0.25 to 1.75
- norm_shift: float32 [512], P('groups'), parts along dimension 0, may hold values from -3 to 3
- up_weight: bfloat16 [512, 1024], P('groups'), parts along dimension 0, may hold values from -0.375 to 0.375
- up_bias: float32 [2048], P('groups'), parts along dimension 0, may hold values from -3 to 3
- down_weight: bfloat16 [2048, 256], P('groups'), parts along dimension 0, may hold values from -0.1875 to 0.1875
- down_bias: float32 [512], P('groups'), parts along dimension 0, may hold values from -3 to 3
- layer_scale: float32 [512], P('groups'), parts along dimension 0, may hold values from 0.5 to 1.5
Outputs:
- block_out: bfloat16 [8, 64, 128, 256], P(('groups', 'rep'), 'rows'), parts along dimension 0
- image_grad: bfloat16 [8, 64, 128, 256], P(('groups', 'rep'), 'rows'), parts along dimension 0
- row_taps_grad: float32 [102, 256], P('groups'), parts along dimension 0
- col_taps_grad: float32 [102, 256], P('groups'), parts along dimension 0
- scale_grad: float32 [512], P('groups'), parts along dimension 0
- down_bias_grad: float32 [512], P('groups'), parts along dimension 0
- down_grad: float32 [2048, 256], P('groups'), parts along dimension 0
- up_bias_grad: float32 [2048], P('groups'), parts along dimension 0
- up_grad: float32 [512, 1024], P('groups'), parts along dimension 0
- gain_grad: float32 [512], P('groups'), parts along dimension 0
- shift_grad: float32 [512], P('groups'), parts along dimension 0
There are 2 independent parts, one for each index of `groups`. A program takes and returns all parts, laid end to end along the dimension named above; each array names one. Nothing has to cross between parts.
All inputs are finite; a program needn't handle non-finite values.
Results may differ from a plain program's by a relative error of at most 0.0086.
Values may be sent and summed in bfloat16 or wider, within the bound.
No kernel may reach another device: no remote copies, remote signals or barrier semaphores. Data moves between devices by JAX's collectives and lax.ppermute only.
A program may use at most 64 MiB of HBM per device.

v0:
```python
import math
import jax
import jax.numpy as jnp
from jax import lax
from jax.sharding import PartitionSpec as P

EPSILON = 1e-06
CUBIC_TERM = 0.044715
TANH_SCALE = 0.7978845608028654


def activate(pre_act):
    return (
        0.5
        * pre_act
        * (1.0 + jnp.tanh(TANH_SCALE * (pre_act + CUBIC_TERM * pre_act * pre_act * pre_act)))
    )


def activate_slope(pre_act):
    inner = jnp.tanh(TANH_SCALE * (pre_act + CUBIC_TERM * pre_act * pre_act * pre_act))
    return 0.5 * (1.0 + inner) + 0.5 * pre_act * (1.0 - inner * inner) * TANH_SCALE * (
        1.0 + 3.0 * CUBIC_TERM * pre_act * pre_act
    )


def pad_along(source, direction, half_reach):
    widths = [(0, 0)] * source.ndim
    widths[direction] = (half_reach, half_reach)
    return jnp.pad(source, widths)


def slide_padded(padded, taps_table, direction, length):
    shape_out = padded.shape[:direction] + (length,) + padded.shape[direction + 1 :]
    result = jnp.zeros(shape_out, jnp.float32)
    for offset in range(taps_table.shape[0]):
        result = result + taps_table[offset] * lax.slice_in_dim(
            padded, offset, offset + length, axis=direction
        ).astype(jnp.float32)
    return result


def tap_sums(cot_field, padded, taps_count, direction):
    length = cot_field.shape[direction]
    lead_axes = tuple(range(cot_field.ndim - 1))
    return jnp.stack(
        [
            jnp.sum(
                cot_field.astype(jnp.float32)
                * lax.slice_in_dim(padded, offset, offset + length, axis=direction).astype(
                    jnp.float32
                ),
                axis=lead_axes,
            )
            for offset in range(taps_count)
        ]
    )


def pointwise(
    mix_rows,
    image_rows,
    cot_rows,
    norm_gain,
    norm_shift,
    up_weight,
    up_bias,
    down_weight,
    down_bias,
    layer_scale,
):
    mix_float = mix_rows.astype(jnp.float32)
    centered = mix_float - jnp.mean(mix_float, axis=-1, keepdims=True)
    inv_dev = lax.rsqrt(jnp.mean(centered * centered, axis=-1, keepdims=True) + EPSILON)
    standardized = centered * inv_dev
    normed = (standardized * norm_gain + norm_shift).astype(jnp.bfloat16)
    pre_act = jnp.dot(normed, up_weight, preferred_element_type=jnp.float32) + up_bias
    activated = activate(pre_act).astype(jnp.bfloat16)
    branch = jnp.dot(activated, down_weight, preferred_element_type=jnp.float32) + down_bias
    cot_float = cot_rows.astype(jnp.float32)
    block_rows = (image_rows.astype(jnp.float32) + layer_scale * branch).astype(jnp.bfloat16)
    branch_cot = cot_float * layer_scale
    branch_grad = branch_cot.astype(jnp.bfloat16)
    act_cot = lax.dot_general(
        branch_grad, down_weight, (((1,), (1,)), ((), ())), preferred_element_type=jnp.float32
    )
    pre_cot = act_cot * activate_slope(pre_act)
    pre_grad = pre_cot.astype(jnp.bfloat16)
    normed_cot = lax.dot_general(
        pre_grad, up_weight, (((1,), (1,)), ((), ())), preferred_element_type=jnp.float32
    )
    scaled_cot = normed_cot * norm_gain
    grad_rows = (
        inv_dev
        * (
            scaled_cot
            - jnp.mean(scaled_cot, axis=-1, keepdims=True)
            - standardized * jnp.mean(scaled_cot * standardized, axis=-1, keepdims=True)
        )
    ).astype(jnp.bfloat16)
    partials = (
        jnp.sum(cot_float * branch, axis=0),
        jnp.sum(branch_cot, axis=0),
        lax.dot_general(
            activated, branch_grad, (((0,), (0,)), ((), ())), preferred_element_type=jnp.float32
        ),
        jnp.sum(pre_cot, axis=0),
        lax.dot_general(
            normed, pre_grad, (((0,), (0,)), ((), ())), preferred_element_type=jnp.float32
        ),
        jnp.sum(normed_cot * standardized, axis=0),
        jnp.sum(normed_cot, axis=0),
    )
    return (block_rows, grad_rows, partials)


def to_columns(band):
    count = lax.axis_size("rows")
    tiles, rows, width, chans = band.shape
    split = band.reshape(tiles, rows, count, width // count, chans).transpose(2, 0, 1, 3, 4)
    split = lax.all_to_all(split, "rows", 0, 0, tiled=True)
    return split.transpose(1, 0, 2, 3, 4).reshape(tiles, count * rows, width // count, chans)


def per_device(
    images,
    cotangent,
    row_taps,
    col_taps,
    norm_gain,
    norm_shift,
    up_weight,
    up_bias,
    down_weight,
    down_bias,
    layer_scale,
):
    tiles_here, band_rows, columns, channels = images.shape
    taps_count = row_taps.shape[0]
    half_reach = (taps_count - 1) // 2
    pixel_scale = 1.0 / math.sqrt(
        tiles_here * lax.axis_size("rep") * band_rows * lax.axis_size("rows") * columns
    )
    bands = 2 if band_rows % 2 == 0 else 1
    band_step = band_rows // bands
    band_pieces = []
    for band in range(bands):
        image_padded = pad_along(
            images[:, band * band_step : (band + 1) * band_step].astype(jnp.float32), 2, half_reach
        )
        row_mix = slide_padded(image_padded, row_taps, 2, columns).astype(jnp.bfloat16)
        row_mix = lax.optimization_barrier(row_mix)
        band_pieces.append(to_columns(row_mix))
    mix_columns = jnp.stack(
        [
            piece.reshape(tiles_here, lax.axis_size("rows"), band_step, piece.shape[2], channels)
            for piece in band_pieces
        ],
        axis=2,
    ).reshape(
        tiles_here, band_rows * lax.axis_size("rows"), columns // lax.axis_size("rows"), channels
    )
    mix_padded = pad_along(mix_columns.astype(jnp.float32), 1, half_reach)
    strip = mix_columns.shape[2]
    parts = 2 if strip % 16 == 0 else 1
    step = strip // parts
    pieces = []
    for part in range(parts):
        local = slide_padded(
            mix_padded[:, :, part * step : (part + 1) * step], col_taps, 1, mix_columns.shape[1]
        ).astype(jnp.bfloat16)
        pieces.append(lax.all_to_all(local, "rows", split_axis=1, concat_axis=2, tiled=True))
    count = lax.axis_size("rows")
    col_mix = jnp.stack(
        [piece.reshape(tiles_here, band_rows, count, step, channels) for piece in pieces], axis=3
    ).reshape(images.shape)
    col_mix = lax.optimization_barrier(col_mix)
    block_rows, grad_rows, partials = pointwise(
        col_mix.reshape(-1, channels),
        images.reshape(-1, channels),
        cotangent.reshape(-1, channels),
        norm_gain,
        norm_shift,
        up_weight,
        up_bias,
        down_weight,
        down_bias,
        layer_scale,
    )
    scale_part, down_bias_part, down_part, up_bias_part, up_part, gain_part, shift_part = partials
    block_out = block_rows.reshape(images.shape)
    grad_rows = lax.optimization_barrier(grad_rows)
    col_grad = grad_rows.reshape(images.shape)
    grad_columns = to_columns(col_grad)
    grad_float = grad_columns.astype(jnp.float32)
    col_part = tap_sums(grad_float, mix_padded, taps_count, 1)
    row_local = slide_padded(
        pad_along(grad_float, 1, half_reach), col_taps[::-1], 1, grad_columns.shape[1]
    ).astype(jnp.bfloat16)
    row_grad = lax.all_to_all(row_local, "rows", split_axis=1, concat_axis=2, tiled=True)
    row_grad = lax.optimization_barrier(row_grad)
    row_part = tap_sums(row_grad, pad_along(images, 2, half_reach), taps_count, 2)
    row_part, row_grad = lax.optimization_barrier((row_part, row_grad))
    image_grad = (
        cotangent.astype(jnp.float32)
        + slide_padded(pad_along(row_grad, 2, half_reach), row_taps[::-1], 2, columns)
    ).astype(jnp.bfloat16)
    down_total, up_total = lax.optimization_barrier(
        lax.psum((down_part * pixel_scale, up_part * pixel_scale), ("rows", "rep"))
    )
    small = (row_part, col_part, scale_part, down_bias_part, up_bias_part, gain_part, shift_part)
    (
        row_total,
        col_total,
        scale_total,
        down_bias_total,
        up_bias_total,
        gain_total,
        shift_total,
    ), image_grad = exchange_sum(
        tuple((part * pixel_scale for part in small)), ("rows", "rep"), image_grad
    )
    return (
        block_out,
        image_grad,
        row_total,
        col_total,
        scale_total,
        down_bias_total,
        down_total,
        up_bias_total,
        up_total,
        gain_total,
        shift_total,
    )


def exchange_sum(parts, axes, companion):
    count = 1
    for axis in axes:
        count *= lax.axis_size(axis)
    stacked = jnp.concatenate([part.reshape(-1, 128) for part in parts])
    piece = -(-stacked.shape[0] // count)
    stacked = jnp.pad(stacked, ((0, piece * count - stacked.shape[0]), (0, 0)))
    spread = lax.all_to_all(stacked.reshape(count, piece, 128), axes, 0, 0, tiled=True)
    mine = jnp.sum(spread, axis=0, keepdims=True)
    mine, companion = lax.optimization_barrier((mine, companion))
    whole = lax.all_to_all(jnp.broadcast_to(mine, (count, piece, 128)), axes, 0, 0, tiled=True)
    return (split_like(whole.reshape(-1), parts), companion)


def split_like(flat, parts):
    out = []
    at = 0
    for part in parts:
        out.append(flat[at : at + part.size].reshape(part.shape))
        at += part.size
    return tuple(out)


def solution(mesh):
    placed = (
        P(("groups", "rep"), "rows", None, None),
        P(("groups", "rep"), "rows", None, None),
        P("groups", None),
        P("groups", None),
        P("groups"),
        P("groups"),
        P("groups", None),
        P("groups"),
        P("groups", None),
        P("groups"),
        P("groups"),
    )
    return jax.shard_map(
        per_device,
        mesh=mesh,
        in_specs=placed,
        out_specs=(
            P(("groups", "rep"), "rows", None, None),
            P(("groups", "rep"), "rows", None, None),
            P("groups", None),
            P("groups", None),
            P("groups"),
            P("groups"),
            P("groups", None),
            P("groups"),
            P("groups", None),
            P("groups"),
            P("groups"),
        ),
        check_vma=False,
    )
```

profile of v0, /device:TPU:0, one launch (start us, length us, event | category | flops | bytes accessed | tf_op | source)
XLA Modules:
  0.0 237.0 jit_solution(5064997916751183123)
XLA Ops:
  11.6 8.1 %fusion.366 = bf16[1,8,128,256]{3,2,1,0:T(8,128)(2,1)S(1)} fusion(f32[1,8,128,256]{3,2,1,0:T(8,128)S(1)} %get-tuple-element.133, f32[256]{0:T(256)S(1)} %bitcast.469, f32[256]{0:T(256)S(1)} %bitcast.472, f32[256]{0:T(256)S(1)} %bitcast.382, f32[256]{0:T(256)S(1)} %bitcast.385, f32[256]{0:T(256)S(1)} %bitcast.388, f32[256]{0:T(256)S(1)} %bitcast.391, ...), kind=kLoop, calls=%fused_computation.834 | loop fusion | flops 26738688 | bytes 1625088 | tf_op jit(solution)/shard_map/convert_element_type | solution.py:151
  20.5 4.4 %all-to-all-start = ((bf16[4,1,8,32,256]{4,3,2,1,0:T(8,128)(2,1)}), bf16[4,1,8,32,256]{4,3,2,1,0:T(8,128)(2,1)S(1)}, u32[]{:S(2)}, u32[]{:S(2)}) async-start(bf16[4,1,8,32,256]{4,3,2,1,0:T(8,128)(2,1)} %copy.28), calls=%async_computation | async-start | bytes 1048576 | tf_op jit(solution)/shard_map/all_to_all | solution.py:121
  24.9 7.9 %fusion.467 = bf16[1,8,128,256]{3,2,1,0:T(8,128)(2,1)S(1)} fusion(f32[1,8,128,256]{3,2,1,0:T(8,128)S(1)} %get-tuple-element.134, f32[256]{0:T(256)S(1)} %bitcast.470, f32[256]{0:T(256)S(1)} %bitcast.473, f32[256]{0:T(256)S(1)} %bitcast.383, f32[256]{0:T(256)S(1)} %bitcast.386, f32[256]{0:T(256)S(1)} %bitcast.389, f32[256]{0:T(256)S(1)} %bitcast.392, ...), kind=kLoop, calls=%fused_computation.935 | loop fusion | flops 26738688 | bytes 1625088 | tf_op jit(solution)/shard_map/convert_element_type | solution.py:151
  37.9 8.2 %all-to-all-done.1 = bf16[4,1,8,32,256]{4,3,2,1,0:T(8,128)(2,1)S(1)} async-done(((bf16[4,1,8,32,256]{4,3,2,1,0:T(8,128)(2,1)}), bf16[4,1,8,32,256]{4,3,2,1,0:T(8,128)(2,1)S(1)}, u32[]{:S(2)}, u32[]{:S(2)}) %all-to-all-start.1) | async-done | bytes 524320 | tf_op jit(solution)/shard_map/all_to_all | solution.py:121
  48.1 9.0 %fusion.676 = bf16[1,64,16,256]{3,2,0,1:T(8,128)(2,1)} fusion(f32[1,64,32,256]{3,2,1,0:T(8,128)S(1)} %bitcast.296, f32[256]{0:T(256)S(1)} %bitcast.623, f32[256]{0:T(256)S(1)} %bitcast.626, f32[256]{0:T(256)S(1)} %bitcast.478, f32[256]{0:T(256)S(1)} %bitcast.481, f32[256]{0:T(256)S(1)} %bitcast.484, f32[256]{0:T(256)S(1)} %bitcast.487, ...), kind=kLoop, calls=%fused_computation.1152 | loop fusion | flops 26738688 | bytes 3722240 | tf_op jit(solution)/shard_map/convert_element_type | solution.py:171
  60.7 9.7 %fusion.677 = bf16[1,64,16,256]{3,2,0,1:T(8,128)(2,1)} fusion(f32[1,64,32,256]{3,2,1,0:T(8,128)S(1)} %bitcast.297, f32[256]{0:T(256)} %bitcast.622, f32[256]{0:T(256)} %bitcast.625, f32[256]{0:T(256)S(1)} %bitcast.479, f32[256]{0:T(256)S(1)} %bitcast.482, f32[256]{0:T(256)S(1)} %bitcast.485, f32[256]{0:T(256)S(1)} %bitcast.488, f32[256]{0:T(256)S(1)} %bitcast.491, ...), kind=kLoop, calls=%fused_computation.1153 | loop fusion | flops 26738688 | bytes 3722240 | tf_op jit(solution)/shard_map/convert_element_type | solution.py:171
  70.4 4.3 %all-to-all-start.3 = ((bf16[1,64,16,256]{3,2,0,1:T(8,128)(2,1)}), bf16[1,64,16,256]{3,2,0,1:T(8,128)(2,1)}, u32[]{:S(2)}, u32[]{:S(2)}) async-start(bf16[1,64,16,256]{3,2,0,1:T(8,128)(2,1)} %fusion.677), calls=%async_computation.3 | async-start | bytes 1048576 | tf_op jit(solution)/shard_map/all_to_all | solution.py:172
  76.8 6.7 %all-to-all-done.3 = bf16[1,64,16,256]{3,2,0,1:T(8,128)(2,1)} async-done(((bf16[1,64,16,256]{3,2,0,1:T(8,128)(2,1)}), bf16[1,64,16,256]{3,2,0,1:T(8,128)(2,1)}, u32[]{:S(2)}, u32[]{:S(2)}) %all-to-all-start.3) | async-done | bytes 524320 | tf_op jit(solution)/shard_map/all_to_all | solution.py:172
  95.3 6.4 %fusion.687 = (f32[1024]{0:T(1024)S(1)}, bf16[2048,1024]{1,0:T(8,128)(2,1)S(1)}) fusion(f32[2048,1024]{1,0:T(8,128)S(1)} %get-tuple-element.246, f32[1024]{0:T(1024)S(1)} %copy-done.19, bf16[2048,256]{1,0:T(8,128)(2,1)S(1)} %get-tuple-element.132, bf16[1024,256]{1,0:T(8,128)(2,1)S(1)} %copy-done.18), kind=kOutput, calls=%fused_computation.1174 | convolution fusion | flops 1117780992 | bytes 14163968 | tf_op jit(solution)/shard_map/dot_general | solution.py:84
  106.0 4.3 %all-to-all-start.4 = ((bf16[4,1,16,32,256]{4,3,2,1,0:T(8,128)(2,1)}), bf16[4,1,16,32,256]{4,3,2,1,0:T(8,128)(2,1)}, u32[]{:S(2)}, u32[]{:S(2)}) async-start(bf16[4,1,16,32,256]{4,3,2,1,0:T(8,128)(2,1)} %bitcast.316), calls=%async_computation.4 | async-start | bytes 2097152 | tf_op jit(solution)/shard_map/all_to_all | solution.py:121
  110.5 4.8 %fusion.268 = f32[256,1024]{1,0:T(8,128)} fusion(bf16[2048,256]{1,0:T(8,128)(2,1)} %copy-done.7, bf16[2048,1024]{1,0:T(8,128)(2,1)} %copy-done.21), kind=kOutput, calls=%fused_computation.736 | convolution fusion | flops 1074003968 | bytes 6291456 | tf_op jit(solution)/shard_map/dot_general | solution.py:108
  116.0 8.8 %all-to-all-done.4 = bf16[4,1,16,32,256]{4,3,2,1,0:T(8,128)(2,1)} async-done(((bf16[4,1,16,32,256]{4,3,2,1,0:T(8,128)(2,1)}), bf16[4,1,16,32,256]{4,3,2,1,0:T(8,128)(2,1)}, u32[]{:S(2)}, u32[]{:S(2)}) %all-to-all-start.4) | async-done | bytes 1048608 | tf_op jit(solution)/shard_map/all_to_all | solution.py:121
  126.2 17.4 %fusion.675 = bf16[1,64,32,256]{3,2,0,1:T(8,128)(2,1)} fusion(f32[1,64,32,256]{3,2,1,0:T(8,128)S(1)} %bitcast.302, f32[256]{0:T(256)S(1)} %bitcast.477, f32[256]{0:T(256)S(1)} %bitcast.534, f32[256]{0:T(256)S(1)} %bitcast.591, f32[256]{0:T(256)S(1)} %bitcast.621, f32[256]{0:T(256)S(1)} %bitcast.618, f32[256]{0:T(256)S(1)} %bitcast.615, ...), kind=kLoop, calls=%fused_computation.1149 | loop fusion | flops 53477376 | bytes 3197952 | tf_op jit(solution)/shard_map/convert_element_type | solution.py:199
  143.6 4.1 %fusion.257 = (f32[256]{0:T(256)S(1)}, f32[256]{0:T(256)S(1)}, f32[256]{0:T(256)S(1)}, f32[256]{0:T(256)S(1)}, f32[256]{0:T(256)S(1)}, /*index=5*/f32[256]{0:T(2...) fusion(f32[1,64,32,256]{3,2,1,0:T(8,128)S(1)} %bitcast.303, ...), kind=kLoop, calls=%fused_computation.712 | loop fusion | flops 18869760 | bytes 4212736 | tf_op jit(solution)/shard_map/reduce_sum | solution.py:48
  147.8 4.9 %fusion.221 = (f32[256]{0:T(256)S(1)}, f32[256]{0:T(256)S(1)}, f32[256]{0:T(256)S(1)}, f32[256]{0:T(256)S(1)}, f32[256]{0:T(256)S(1)}, /*index=5*/f32[256]{0:T(2...) fusion(f32[1,64,32,256]{3,2,1,0:T(8,128)S(1)} %bitcast.304, ...), kind=kLoop, calls=%fused_computation.676 | loop fusion | flops 18869760 | bytes 4212736 | tf_op jit(solution)/shard_map/reduce_sum | solution.py:48
  152.6 4.5 %all-to-all-start.5 = ((bf16[1,64,32,256]{3,2,0,1:T(8,128)(2,1)}), bf16[1,64,32,256]{3,2,0,1:T(8,128)(2,1)}, u32[]{:S(2)}, u32[]{:S(2)}) async-start(bf16[1,64,32,256]{3,2,0,1:T(8,128)(2,1)} %fusion.675), calls=%async_computation.5 | async-start | bytes 2097152 | tf_op jit(solution)/shard_map/all_to_all | solution.py:200
  157.2 9.8 %fusion.185 = (f32[256]{0:T(256)S(1)}, f32[256]{0:T(256)S(1)}, f32[256]{0:T(256)S(1)}, f32[256]{0:T(256)S(1)}, f32[256]{0:T(256)S(1)}, /*index=5*/f32[256]{0:T(2...) fusion(f32[1,64,32,256]{3,2,1,0:T(8,128)} %bitcast.305, ...), kind=kLoop, calls=%fused_computation.640 | loop fusion | flops 14676480 | bytes 4208640 | tf_op jit(solution)/shard_map/reduce_sum | solution.py:48
  172.8 4.8 %fusion.56 = (f32[256]{0:T(256)S(1)}, f32[256]{0:T(256)S(1)}, f32[256]{0:T(256)S(1)}, f32[256]{0:T(256)S(1)}, f32[256]{0:T(256)S(1)}, /*index=5*/f32[256]{0:T(25...) fusion(bf16[1,16,128,256]{3,2,1,0:T(8,128)(2,1)S(1)} %bitcast.3, ...), kind=kLoop, calls=%fused_computation.511 | loop fusion | flops 28831232 | bytes 2115584 | tf_op jit(solution)/shard_map/reduce_sum | solution.py:48
  177.6 5.1 %fusion.55 = (f32[256]{0:T(256)S(1)}, f32[256]{0:T(256)S(1)}, f32[256]{0:T(256)S(1)}, f32[256]{0:T(256)S(1)}, f32[256]{0:T(256)S(1)}, /*index=5*/f32[256]{0:T(25...) fusion(bf16[1,16,128,256]{3,2,1,0:T(8,128)(2,1)S(1)} %bitcast.3, ...), kind=kLoop, calls=%fused_computation.510 | loop fusion | flops 28831232 | bytes 2115584 | tf_op jit(solution)/shard_map/reduce_sum | solution.py:48
  182.7 4.2 %fusion.54 = (f32[256]{0:T(256)S(1)}, f32[256]{0:T(256)S(1)}, f32[256]{0:T(256)S(1)}, f32[256]{0:T(256)S(1)}, f32[256]{0:T(256)S(1)}, /*index=5*/f32[256]{0:T(25...) fusion(bf16[1,16,128,256]{3,2,1,0:T(8,128)(2,1)S(1)} %bitcast.3, ...), kind=kLoop, calls=%fused_computation.509 | loop fusion | flops 24113408 | bytes 2112512 | tf_op jit(solution)/shard_map/reduce_sum | solution.py:48
  188.0 6.5 %all-to-all-start.6 = ((f32[16,14,128]{2,1,0:T(8,128)}), f32[16,14,128]{2,1,0:T(8,128)S(1)}, u32[]{:S(2)}, u32[]{:S(2)}) async-start(f32[16,14,128]{2,1,0:T(8,128)} %reshape.804), calls=%async_computation.6 | async-start | bytes 262144 | tf_op jit(solution)/shard_map/all_to_all | solution.py:245
  194.5 16.5 %fusion.259 = bf16[1,16,128,256]{3,2,1,0:T(8,128)(2,1)} fusion(bf16[1,16,128,256]{3,2,1,0:T(8,128)(2,1)S(1)} %copy-done.5, bf16[1,16,128,256]{3,2,1,0:T(8,128)(2,1)S(1)} %bitcast.309, f32[256]{0:T(256)S(1)} %bitcast.381, f32[256]{0:T(256)S(1)} %bitcast.324, f32[256]{0:T(256)S(1)} %bitcast.438, f32[256]{0:T(256)S(1)} %bitcast.468, f32[256]{0:T(256)S(1)} %bitcast.465, ...), kind=kLoop, calls=%fused_computation.718 | loop fusion | flops 81264640 | bytes 3197952 | tf_op jit(solution)/shard_map/convert_element_type | solution.py:207
  211.7 6.0 %all-to-all-start.7 = ((f32[16,14,128]{2,1,0:T(8,128)}), f32[16,14,128]{2,1,0:T(8,128)S(1)}, u32[]{:S(2)}, u32[]{:S(2)}) async-start(f32[16,14,128]{2,1,0:T(8,128)} %broadcast_in_dim.8), calls=%async_computation.7 | async-start | bytes 262144 | tf_op jit(solution)/shard_map/all_to_all | solution.py:248
  217.7 7.3 %all-to-all-done.7 = f32[16,14,128]{2,1,0:T(8,128)S(1)} async-done(((f32[16,14,128]{2,1,0:T(8,128)}), f32[16,14,128]{2,1,0:T(8,128)S(1)}, u32[]{:S(2)}, u32[]{:S(2)}) %all-to-all-start.7) | async-done | bytes 114720 | tf_op jit(solution)/shard_map/all_to_all | solution.py:248
  (102 shorter events, 48.8 us)
Async XLA Ops:
  7.2 79.3 %copy-start = (bf16[256,1024]{1,0:T(8,128)(2,1)S(1)}, bf16[256,1024]{1,0:T(8,128)(2,1)}, u32[]{:S(2)}) copy-start(bf16[256,1024]{1,0:T(8,128)(2,1)} %param.17) | copy-start | bytes 1572868
  20.5 13.2 %copy-start.9 = (f32[51,256]{1,0:T(8,128)S(1)}, f32[51,256]{1,0:T(8,128)}, u32[]{:S(2)}) copy-start(f32[51,256]{1,0:T(8,128)} %param.14) | copy-start | bytes 156676
  20.5 13.2 %all-to-all-start = ((bf16[4,1,8,32,256]{4,3,2,1,0:T(8,128)(2,1)}), bf16[4,1,8,32,256]{4,3,2,1,0:T(8,128)(2,1)S(1)}, u32[]{:S(2)}, u32[]{:S(2)}) async-start(bf16[4,1,8,32,256]{4,3,2,1,0:T(8,128)(2,1)} %copy.28), calls=%async_computation | async-start | bytes 1048576 | tf_op jit(solution)/shard_map/all_to_all | solution.py:121
  33.7 12.4 %all-to-all-start.1 = ((bf16[4,1,8,32,256]{4,3,2,1,0:T(8,128)(2,1)}), bf16[4,1,8,32,256]{4,3,2,1,0:T(8,128)(2,1)S(1)}, u32[]{:S(2)}, u32[]{:S(2)}) async-start(bf16[4,1,8,32,256]{4,3,2,1,0:T(8,128)(2,1)} %copy.29), calls=%async_computation.1 | async-start | bytes 1048576 | tf_op jit(solution)/shard_map/all_to_all | solution.py:121
  46.1 2.0 copy-start.12
  57.2 13.2 %all-to-all-start.2 = ((bf16[1,64,16,256]{3,2,0,1:T(8,128)(2,1)}), bf16[1,64,16,256]{3,2,0,1:T(8,128)(2,1)S(1)}, u32[]{:S(2)}, u32[]{:S(2)}) async-start(bf16[1,64,16,256]{3,2,0,1:T(8,128)(2,1)} %fusion.676), calls=%async_computation.2 | async-start | bytes 1048576 | tf_op jit(solution)/shard_map/all_to_all | solution.py:172
  70.4 13.1 %all-to-all-start.3 = ((bf16[1,64,16,256]{3,2,0,1:T(8,128)(2,1)}), bf16[1,64,16,256]{3,2,0,1:T(8,128)(2,1)}, u32[]{:S(2)}, u32[]{:S(2)}) async-start(bf16[1,64,16,256]{3,2,0,1:T(8,128)(2,1)} %fusion.677), calls=%async_computation.3 | async-start | bytes 1048576 | tf_op jit(solution)/shard_map/all_to_all | solution.py:172
  86.5 3.8 %copy-start.7 = (bf16[2048,256]{1,0:T(8,128)(2,1)}, bf16[2048,256]{1,0:T(8,128)(2,1)S(1)}, u32[]{:S(2)}) copy-start(bf16[2048,256]{1,0:T(8,128)(2,1)S(1)} %add_convert_fusion) | copy-start | bytes 3145732
  86.5 3.8 %copy-start.2 = (bf16[1,16,128,256]{3,2,1,0:T(8,128)(2,1)S(1)}, bf16[1,16,128,256]{3,2,1,0:T(8,128)(2,1)}, u32[]{:S(2)}) copy-start(bf16[1,16,128,256]{3,2,1,0:T(8,128)(2,1)} %param.11) | copy-start | bytes 3145732
  86.6 3.8 %copy-start.4 = (bf16[1,16,128,256]{3,2,1,0:T(8,128)(2,1)S(1)}, bf16[1,16,128,256]{3,2,1,0:T(8,128)(2,1)}, u32[]{:S(2)}) copy-start(bf16[1,16,128,256]{3,2,1,0:T(8,128)(2,1)} %param.12) | copy-start | bytes 3145732
  86.6 3.8 %copy-start.17 = (f32[256]{0:T(256)S(1)}, f32[256]{0:T(256)}, u32[]{:S(2)}) copy-start(f32[256]{0:T(256)} %param.21) | copy-start | bytes 3076
  86.6 3.8 %copy-start.18 = (bf16[1024,256]{1,0:T(8,128)(2,1)S(1)}, bf16[1024,256]{1,0:T(8,128)(2,1)}, u32[]{:S(2)}) copy-start(bf16[1024,256]{1,0:T(8,128)(2,1)} %param.19) | copy-start | bytes 1572868
  86.6 3.8 %copy-start.20 = (f32[256]{0:T(256)S(1)}, f32[256]{0:T(256)}, u32[]{:S(2)}) copy-start(f32[256]{0:T(256)} %param.20) | copy-start | bytes 3076
  106.0 18.8 %all-to-all-start.4 = ((bf16[4,1,16,32,256]{4,3,2,1,0:T(8,128)(2,1)}), bf16[4,1,16,32,256]{4,3,2,1,0:T(8,128)(2,1)}, u32[]{:S(2)}, u32[]{:S(2)}) async-start(bf16[4,1,16,32,256]{4,3,2,1,0:T(8,128)(2,1)} %bitcast.316), calls=%async_computation.4 | async-start | bytes 2097152 | tf_op jit(solution)/shard_map/all_to_all | solution.py:121
  110.2 107.5 %all-reduce.10.cloned.1.call-start = ((), (), s32[]{:S(2)}) async-start(), calls=%async_computation.8 | async-start | bytes 4194304 | tf_op jit(solution)/shard_map/psum | solution.py:209
  115.3 10.9 %copy-start.11 = (f32[1,256]{1,0:T(1,128)S(1)}, f32[1,256]{1,0:T(1,128)}, u32[]{:S(2)}) copy-start(f32[1,256]{1,0:T(1,128)} %get-tuple-element.190) | copy-start | bytes 3076
  115.3 10.9 %copy-start.13 = (f32[1,256]{1,0:T(1,128)S(1)}, f32[1,256]{1,0:T(1,128)}, u32[]{:S(2)}) copy-start(f32[1,256]{1,0:T(1,128)} %get-tuple-element.191) | copy-start | bytes 3076
  126.2 21.6 %copy-start.1 = (f32[4,1,16,32,256]{4,3,2,0,1:T(8,128)}, f32[4,1,16,32,256]{4,3,2,0,1:T(8,128)S(1)}, u32[]{:S(2)}) copy-start(f32[4,1,16,32,256]{4,3,2,0,1:T(8,128)S(1)} %bitcast_convert_fusion) | copy-start | bytes 6291460
  152.6 18.8 %all-to-all-start.5 = ((bf16[1,64,32,256]{3,2,0,1:T(8,128)(2,1)}), bf16[1,64,32,256]{3,2,0,1:T(8,128)(2,1)}, u32[]{:S(2)}, u32[]{:S(2)}) async-start(bf16[1,64,32,256]{3,2,0,1:T(8,128)(2,1)} %fusion.675), calls=%async_computation.5 | async-start | bytes 2097152 | tf_op jit(solution)/shard_map/all_to_all | solution.py:200
  168.5 4.3 %copy-start.3 = (bf16[1,16,128,256]{3,2,1,0:T(8,128)(2,1)S(1)}, bf16[1,16,128,256]{3,2,1,0:T(8,128)(2,1)}, u32[]{:S(2)}) copy-start(bf16[1,16,128,256]{3,2,1,0:T(8,128)(2,1)} %param.11) | copy-start | bytes 3145732
  186.9 7.7 %copy-start.5 = (bf16[1,16,128,256]{3,2,1,0:T(8,128)(2,1)S(1)}, bf16[1,16,128,256]{3,2,1,0:T(8,128)(2,1)}, u32[]{:S(2)}) copy-start(bf16[1,16,128,256]{3,2,1,0:T(8,128)(2,1)} %param.12) | copy-start | bytes 3145732
  188.0 23.0 %all-to-all-start.6 = ((f32[16,14,128]{2,1,0:T(8,128)}), f32[16,14,128]{2,1,0:T(8,128)S(1)}, u32[]{:S(2)}, u32[]{:S(2)}) async-start(f32[16,14,128]{2,1,0:T(8,128)} %reshape.804), calls=%async_computation.6 | async-start | bytes 262144 | tf_op jit(solution)/shard_map/all_to_all | solution.py:245
  211.7 13.4 %all-to-all-start.7 = ((f32[16,14,128]{2,1,0:T(8,128)}), f32[16,14,128]{2,1,0:T(8,128)S(1)}, u32[]{:S(2)}, u32[]{:S(2)}) async-start(f32[16,14,128]{2,1,0:T(8,128)} %broadcast_in_dim.8), calls=%async_computation.7 | async-start | bytes 262144 | tf_op jit(solution)/shard_map/all_to_all | solution.py:248
  217.7 11.5 %copy-start.8 = (f32[256,1024]{1,0:T(8,128)S(1)}, f32[256,1024]{1,0:T(8,128)}, u32[]{:S(2)}) copy-start(f32[256,1024]{1,0:T(8,128)} %get-tuple-element.266) | copy-start | bytes 3145732
  (7 other events, 9.5 us)
Sparse Core Ops, SparseCore 0:
  115.4 102.0 all-reduce.9
where the time goes:
time: 238 us; the launch traced here: 237 us
  other arithmetic  113 us (47%)
  starting transfers between devices  37.3 us (16%)
  waiting for transfers between devices  33.7 us (14%)
  matrix products  21.7 us (9%)
  local copies, waits for them, and re-layouts  16.3 us (7%)
  between operations  14.6 us (6%)
    reduce_sum x7, other arithmetic, tap_sums(): jnp.sum(cot_field.astype(jnp.float32) * lax.slice_in_dim(padded, offset,...  34.4 us
    convert_element_type x2, other arithmetic, per_device(): local = slide_padded(mix_padded[:, :, part * step:(part + 1) * step], col...  18.8 us
    convert_element_type x1, other arithmetic, per_device(): row_local = slide_padded(pad_along(grad_float, 1, half_reach), col_taps[:...  17.4 us
    all_to_all x3, waiting for transfers between devices, to_columns(): split = lax.all_to_all(split, 'rows', 0, 0, tiled=True)  17 us
    convert_element_type x1, other arithmetic, per_device(): image_grad = (cotangent.astype(jnp.float32) + slide_padded(pad_along(row_...  16.5 us
    convert_element_type x2, other arithmetic, per_device(): slide_padded(image_padded, row_taps, 2, columns).astype(jnp.bfloat16)  16 us
    all_to_all x3, starting transfers between devices, to_columns(): split = lax.all_to_all(split, 'rows', 0, 0, tiled=True)  12.2 us
    all_to_all x2, starting transfers between devices, per_device(): lax.all_to_all(local, 'rows', split_axis=1, concat_axis=2, tiled=True)  7.78 us
  transfers between devices with their start and end apart: 9, of which 5 were waited for; matrix products, arithmetic and copies ran while one was open for 42% of the time, Pallas kernels for 0%

commit v1 on v0

--- a/solution.py
+++ b/solution.py
@@ -169,7 +169,20 @@
         local = slide_padded(
             mix_padded[:, :, part * step : (part + 1) * step], col_taps, 1, mix_columns.shape[1]
         ).astype(jnp.bfloat16)
-        pieces.append(lax.all_to_all(local, "rows", split_axis=1, concat_axis=2, tiled=True))
+
+        def connect_the_works(device_axis, inp):
+            near = jnp.concatenate(
+                jax.lax.all_to_all(
+                    jnp.stack(jnp.split(inp, jax.lax.axis_size(device_axis), axis=1)),
+                    device_axis,
+                    0,
+                    0,
+                ),
+                axis=2,
+            )
+            return near
+
+        pieces.append(connect_the_works("rows", local))
     count = lax.axis_size("rows")
     col_mix = jnp.stack(
         [piece.reshape(tiles_here, band_rows, count, step, channels) for piece in pieces], axis=3

time: 238 us -> 239 us (level)
  no operation moved by 1% of the time
where the time goes in v1:
time: 239 us; the launch traced here: 238 us
  other arithmetic  114 us (48%)
  starting transfers between devices  37.4 us (16%)
  waiting for transfers between devices  33.7 us (14%)
  matrix products  21.5 us (9%)
  local copies, waits for them, and re-layouts  16.5 us (7%)
  between operations  14.6 us (6%)
    reduce_sum x7, other arithmetic, tap_sums(): jnp.sum(cot_field.astype(jnp.float32) * lax.slice_in_dim(padded, offset,...  34.4 us
    convert_element_type x2, other arithmetic, per_device(): local = slide_padded(mix_padded[:, :, part * step:(part + 1) * step], col...  17.5 us
    convert_element_type x1, other arithmetic, per_device(): row_local = slide_padded(pad_along(grad_float, 1, half_reach), col_taps[:...  17.4 us
    all_to_all x3, waiting for transfers between devices, to_columns(): split = lax.all_to_all(split, 'rows', 0, 0, tiled=True)  17 us
    convert_element_type x1, other arithmetic, per_device(): image_grad = (cotangent.astype(jnp.float32) + slide_padded(pad_along(row_...  16.5 us
    convert_element_type x2, other arithmetic, per_device(): slide_padded(image_padded, row_taps, 2, columns).astype(jnp.bfloat16)  16 us
    all_to_all x3, starting transfers between devices, to_columns(): split = lax.all_to_all(split, 'rows', 0, 0, tiled=True)  12.2 us
    all_to_all x2, starting transfers between devices, connect_the_works(): jax.lax.all_to_all(jnp.stack(jnp.split(inp, jax.lax.axis_size(device_axis...  7.78 us
  transfers between devices with their start and end apart: 9, of which 5 were waited for; matrix products, arithmetic and copies ran while one was open for 42% of the time, Pallas kernels for 0%

profile of v1, /device:TPU:0, one launch (start us, length us, event | category | flops | bytes accessed | tf_op | source)
XLA Modules:
  0.0 237.5 jit_solution(13799457777041026401)
XLA Ops:
  11.6 8.1 %fusion.366 = bf16[1,8,128,256]{3,2,1,0:T(8,128)(2,1)S(1)} fusion(f32[1,8,128,256]{3,2,1,0:T(8,128)S(1)} %get-tuple-element.133, f32[256]{0:T(256)S(1)} %bitcast.479, f32[256]{0:T(256)S(1)} %bitcast.482, f32[256]{0:T(256)S(1)} %bitcast.392, f32[256]{0:T(256)S(1)} %bitcast.395, f32[256]{0:T(256)S(1)} %bitcast.398, f32[256]{0:T(256)S(1)} %bitcast.401, ...), kind=kLoop, calls=%fused_computation.834 | loop fusion | flops 26738688 | bytes 1625088 | tf_op jit(solution)/shard_map/convert_element_type | solution.py:151
  20.5 4.4 %all-to-all-start = ((bf16[4,1,8,32,256]{4,3,2,1,0:T(8,128)(2,1)}), bf16[4,1,8,32,256]{4,3,2,1,0:T(8,128)(2,1)S(1)}, u32[]{:S(2)}, u32[]{:S(2)}) async-start(bf16[4,1,8,32,256]{4,3,2,1,0:T(8,128)(2,1)} %copy.38), calls=%async_computation | async-start | bytes 1048576 | tf_op jit(solution)/shard_map/all_to_all | solution.py:121
  24.9 7.9 %fusion.467 = bf16[1,8,128,256]{3,2,1,0:T(8,128)(2,1)S(1)} fusion(f32[1,8,128,256]{3,2,1,0:T(8,128)S(1)} %get-tuple-element.134, f32[256]{0:T(256)S(1)} %bitcast.480, f32[256]{0:T(256)S(1)} %bitcast.483, f32[256]{0:T(256)S(1)} %bitcast.393, f32[256]{0:T(256)S(1)} %bitcast.396, f32[256]{0:T(256)S(1)} %bitcast.399, f32[256]{0:T(256)S(1)} %bitcast.402, ...), kind=kLoop, calls=%fused_computation.935 | loop fusion | flops 26738688 | bytes 1625088 | tf_op jit(solution)/shard_map/convert_element_type | solution.py:151
  37.9 8.2 %all-to-all-done.1 = bf16[4,1,8,32,256]{4,3,2,1,0:T(8,128)(2,1)S(1)} async-done(((bf16[4,1,8,32,256]{4,3,2,1,0:T(8,128)(2,1)}), bf16[4,1,8,32,256]{4,3,2,1,0:T(8,128)(2,1)S(1)}, u32[]{:S(2)}, u32[]{:S(2)}) %all-to-all-start.1) | async-done | bytes 524320 | tf_op jit(solution)/shard_map/all_to_all | solution.py:121
  48.1 8.4 %fusion.674 = bf16[1,64,16,256]{3,2,1,0:T(8,128)(2,1)S(1)} fusion(f32[1,64,32,256]{3,2,1,0:T(8,128)S(1)} %bitcast.306, f32[256]{0:T(256)S(1)} %bitcast.633, f32[256]{0:T(256)S(1)} %bitcast.636, f32[256]{0:T(256)S(1)} %bitcast.488, f32[256]{0:T(256)S(1)} %bitcast.491, f32[256]{0:T(256)S(1)} %bitcast.494, f32[256]{0:T(256)S(1)} %bitcast.497, ...), kind=kLoop, calls=%fused_computation.1148 | loop fusion | flops 26738688 | bytes 3722240 | tf_op jit(solution)/shard_map/convert_element_type | solution.py:171
  61.0 9.1 %fusion.673 = bf16[1,64,16,256]{3,2,1,0:T(8,128)(2,1)S(1)} fusion(f32[1,64,32,256]{3,2,1,0:T(8,128)S(1)} %bitcast.307, f32[256]{0:T(256)} %bitcast.632, f32[256]{0:T(256)} %bitcast.635, f32[256]{0:T(256)S(1)} %bitcast.489, f32[256]{0:T(256)S(1)} %bitcast.492, f32[256]{0:T(256)S(1)} %bitcast.495, f32[256]{0:T(256)S(1)} %bitcast.498, f32[256]{0:T(256)S(1)} %bitcast.501, ...), kind=kLoop, calls=%fused_computation.1147 | loop fusion | flops 26738688 | bytes 3722240 | tf_op jit(solution)/shard_map/convert_element_type | solution.py:171
  71.0 4.3 %all-to-all-start.3 = ((bf16[4,1,16,16,256]{4,3,2,1,0:T(8,128)(2,1)}), bf16[4,1,16,16,256]{4,3,2,1,0:T(8,128)(2,1)}, u32[]{:S(2)}, u32[]{:S(2)}) async-start(bf16[4,1,16,16,256]{4,3,2,1,0:T(8,128)(2,1)} %pad_maximum_fusion.2), calls=%async_computation.3 | async-start | bytes 1048576 | tf_op jit(solution)/shard_map/all_to_all | solution.py:175
  77.4 6.7 %all-to-all-done.3 = bf16[4,1,16,16,256]{4,3,2,1,0:T(8,128)(2,1)} async-done(((bf16[4,1,16,16,256]{4,3,2,1,0:T(8,128)(2,1)}), bf16[4,1,16,16,256]{4,3,2,1,0:T(8,128)(2,1)}, u32[]{:S(2)}, u32[]{:S(2)}) %all-to-all-start.3) | async-done | bytes 524320 | tf_op jit(solution)/shard_map/all_to_all | solution.py:175
  95.8 6.4 %fusion.685 = (f32[1024]{0:T(1024)S(1)}, bf16[2048,1024]{1,0:T(8,128)(2,1)S(1)}) fusion(f32[2048,1024]{1,0:T(8,128)S(1)} %get-tuple-element.254, f32[1024]{0:T(1024)S(1)} %copy-done.19, bf16[2048,256]{1,0:T(8,128)(2,1)S(1)} %get-tuple-element.132, bf16[1024,256]{1,0:T(8,128)(2,1)S(1)} %copy-done.18), kind=kOutput, calls=%fused_computation.1182 | convolution fusion | flops 1117780992 | bytes 14163968 | tf_op jit(solution)/shard_map/dot_general | solution.py:84
  106.4 4.3 %all-to-all-start.4 = ((bf16[4,1,16,32,256]{4,3,2,1,0:T(8,128)(2,1)}), bf16[4,1,16,32,256]{4,3,2,1,0:T(8,128)(2,1)}, u32[]{:S(2)}, u32[]{:S(2)}) async-start(bf16[4,1,16,32,256]{4,3,2,1,0:T(8,128)(2,1)} %bitcast.326), calls=%async_computation.4 | async-start | bytes 2097152 | tf_op jit(solution)/shard_map/all_to_all | solution.py:121
  111.0 4.8 %fusion.268 = f32[256,1024]{1,0:T(8,128)} fusion(bf16[2048,256]{1,0:T(8,128)(2,1)} %copy-done.7, bf16[2048,1024]{1,0:T(8,128)(2,1)} %copy-done.21), kind=kOutput, calls=%fused_computation.736 | convolution fusion | flops 1074003968 | bytes 6291456 | tf_op jit(solution)/shard_map/dot_general | solution.py:108
  116.4 8.8 %all-to-all-done.4 = bf16[4,1,16,32,256]{4,3,2,1,0:T(8,128)(2,1)} async-done(((bf16[4,1,16,32,256]{4,3,2,1,0:T(8,128)(2,1)}), bf16[4,1,16,32,256]{4,3,2,1,0:T(8,128)(2,1)}, u32[]{:S(2)}, u32[]{:S(2)}) %all-to-all-start.4) | async-done | bytes 1048608 | tf_op jit(solution)/shard_map/all_to_all | solution.py:121
  126.7 17.4 %fusion.675 = bf16[1,64,32,256]{3,2,0,1:T(8,128)(2,1)} fusion(f32[1,64,32,256]{3,2,1,0:T(8,128)S(1)} %bitcast.312, f32[256]{0:T(256)S(1)} %bitcast.487, f32[256]{0:T(256)S(1)} %bitcast.544, f32[256]{0:T(256)S(1)} %bitcast.601, f32[256]{0:T(256)S(1)} %bitcast.631, f32[256]{0:T(256)S(1)} %bitcast.628, f32[256]{0:T(256)S(1)} %bitcast.625, ...), kind=kLoop, calls=%fused_computation.1149 | loop fusion | flops 53477376 | bytes 3197952 | tf_op jit(solution)/shard_map/convert_element_type | solution.py:212
  144.1 4.1 %fusion.257 = (f32[256]{0:T(256)S(1)}, f32[256]{0:T(256)S(1)}, f32[256]{0:T(256)S(1)}, f32[256]{0:T(256)S(1)}, f32[256]{0:T(256)S(1)}, /*index=5*/f32[256]{0:T(2...) fusion(f32[1,64,32,256]{3,2,1,0:T(8,128)S(1)} %bitcast.313, ...), kind=kLoop, calls=%fused_computation.712 | loop fusion | flops 18869760 | bytes 4212736 | tf_op jit(solution)/shard_map/reduce_sum | solution.py:48
  148.2 4.9 %fusion.221 = (f32[256]{0:T(256)S(1)}, f32[256]{0:T(256)S(1)}, f32[256]{0:T(256)S(1)}, f32[256]{0:T(256)S(1)}, f32[256]{0:T(256)S(1)}, /*index=5*/f32[256]{0:T(2...) fusion(f32[1,64,32,256]{3,2,1,0:T(8,128)S(1)} %bitcast.314, ...), kind=kLoop, calls=%fused_computation.676 | loop fusion | flops 18869760 | bytes 4212736 | tf_op jit(solution)/shard_map/reduce_sum | solution.py:48
  153.1 4.5 %all-to-all-start.5 = ((bf16[1,64,32,256]{3,2,0,1:T(8,128)(2,1)}), bf16[1,64,32,256]{3,2,0,1:T(8,128)(2,1)}, u32[]{:S(2)}, u32[]{:S(2)}) async-start(bf16[1,64,32,256]{3,2,0,1:T(8,128)(2,1)} %fusion.675), calls=%async_computation.5 | async-start | bytes 2097152 | tf_op jit(solution)/shard_map/all_to_all | solution.py:213
  157.6 9.8 %fusion.185 = (f32[256]{0:T(256)S(1)}, f32[256]{0:T(256)S(1)}, f32[256]{0:T(256)S(1)}, f32[256]{0:T(256)S(1)}, f32[256]{0:T(256)S(1)}, /*index=5*/f32[256]{0:T(2...) fusion(f32[1,64,32,256]{3,2,1,0:T(8,128)} %bitcast.315, ...), kind=kLoop, calls=%fused_computation.640 | loop fusion | flops 14676480 | bytes 4208640 | tf_op jit(solution)/shard_map/reduce_sum | solution.py:48
  173.2 4.8 %fusion.56 = (f32[256]{0:T(256)S(1)}, f32[256]{0:T(256)S(1)}, f32[256]{0:T(256)S(1)}, f32[256]{0:T(256)S(1)}, f32[256]{0:T(256)S(1)}, /*index=5*/f32[256]{0:T(25...) fusion(bf16[1,16,128,256]{3,2,1,0:T(8,128)(2,1)S(1)} %bitcast.3, ...), kind=kLoop, calls=%fused_computation.511 | loop fusion | flops 28831232 | bytes 2115584 | tf_op jit(solution)/shard_map/reduce_sum | solution.py:48
  178.0 5.1 %fusion.55 = (f32[256]{0:T(256)S(1)}, f32[256]{0:T(256)S(1)}, f32[256]{0:T(256)S(1)}, f32[256]{0:T(256)S(1)}, f32[256]{0:T(256)S(1)}, /*index=5*/f32[256]{0:T(25...) fusion(bf16[1,16,128,256]{3,2,1,0:T(8,128)(2,1)S(1)} %bitcast.3, ...), kind=kLoop, calls=%fused_computation.510 | loop fusion | flops 28831232 | bytes 2115584 | tf_op jit(solution)/shard_map/reduce_sum | solution.py:48
  183.2 4.2 %fusion.54 = (f32[256]{0:T(256)S(1)}, f32[256]{0:T(256)S(1)}, f32[256]{0:T(256)S(1)}, f32[256]{0:T(256)S(1)}, f32[256]{0:T(256)S(1)}, /*index=5*/f32[256]{0:T(25...) fusion(bf16[1,16,128,256]{3,2,1,0:T(8,128)(2,1)S(1)} %bitcast.3, ...), kind=kLoop, calls=%fused_computation.509 | loop fusion | flops 24113408 | bytes 2112512 | tf_op jit(solution)/shard_map/reduce_sum | solution.py:48
  188.4 6.6 %all-to-all-start.6 = ((f32[16,14,128]{2,1,0:T(8,128)}), f32[16,14,128]{2,1,0:T(8,128)S(1)}, u32[]{:S(2)}, u32[]{:S(2)}) async-start(f32[16,14,128]{2,1,0:T(8,128)} %reshape.810), calls=%async_computation.6 | async-start | bytes 262144 | tf_op jit(solution)/shard_map/all_to_all | solution.py:258
  195.0 16.5 %fusion.259 = bf16[1,16,128,256]{3,2,1,0:T(8,128)(2,1)} fusion(bf16[1,16,128,256]{3,2,1,0:T(8,128)(2,1)S(1)} %copy-done.5, bf16[1,16,128,256]{3,2,1,0:T(8,128)(2,1)S(1)} %bitcast.319, f32[256]{0:T(256)S(1)} %bitcast.391, f32[256]{0:T(256)S(1)} %bitcast.334, f32[256]{0:T(256)S(1)} %bitcast.448, f32[256]{0:T(256)S(1)} %bitcast.478, f32[256]{0:T(256)S(1)} %bitcast.475, ...), kind=kLoop, calls=%fused_computation.718 | loop fusion | flops 81264640 | bytes 3197952 | tf_op jit(solution)/shard_map/convert_element_type | solution.py:220
  212.2 6.0 %all-to-all-start.7 = ((f32[16,14,128]{2,1,0:T(8,128)}), f32[16,14,128]{2,1,0:T(8,128)S(1)}, u32[]{:S(2)}, u32[]{:S(2)}) async-start(f32[16,14,128]{2,1,0:T(8,128)} %broadcast_in_dim.8), calls=%async_computation.7 | async-start | bytes 262144 | tf_op jit(solution)/shard_map/all_to_all | solution.py:261
  218.2 7.3 %all-to-all-done.7 = f32[16,14,128]{2,1,0:T(8,128)S(1)} async-done(((f32[16,14,128]{2,1,0:T(8,128)}), f32[16,14,128]{2,1,0:T(8,128)S(1)}, u32[]{:S(2)}, u32[]{:S(2)}) %all-to-all-start.7) | async-done | bytes 114720 | tf_op jit(solution)/shard_map/all_to_all | solution.py:261
  (106 shorter events, 50.5 us)
Async XLA Ops:
  7.2 79.9 %copy-start = (bf16[256,1024]{1,0:T(8,128)(2,1)S(1)}, bf16[256,1024]{1,0:T(8,128)(2,1)}, u32[]{:S(2)}) copy-start(bf16[256,1024]{1,0:T(8,128)(2,1)} %param.17) | copy-start | bytes 1572868
  20.5 13.2 %copy-start.9 = (f32[51,256]{1,0:T(8,128)S(1)}, f32[51,256]{1,0:T(8,128)}, u32[]{:S(2)}) copy-start(f32[51,256]{1,0:T(8,128)} %param.14) | copy-start | bytes 156676
  20.5 13.2 %all-to-all-start = ((bf16[4,1,8,32,256]{4,3,2,1,0:T(8,128)(2,1)}), bf16[4,1,8,32,256]{4,3,2,1,0:T(8,128)(2,1)S(1)}, u32[]{:S(2)}, u32[]{:S(2)}) async-start(bf16[4,1,8,32,256]{4,3,2,1,0:T(8,128)(2,1)} %copy.38), calls=%async_computation | async-start | bytes 1048576 | tf_op jit(solution)/shard_map/all_to_all | solution.py:121
  33.7 12.4 %all-to-all-start.1 = ((bf16[4,1,8,32,256]{4,3,2,1,0:T(8,128)(2,1)}), bf16[4,1,8,32,256]{4,3,2,1,0:T(8,128)(2,1)S(1)}, u32[]{:S(2)}, u32[]{:S(2)}) async-start(bf16[4,1,8,32,256]{4,3,2,1,0:T(8,128)(2,1)} %copy.39), calls=%async_computation.1 | async-start | bytes 1048576 | tf_op jit(solution)/shard_map/all_to_all | solution.py:121
  46.1 2.0 copy-start.12
  57.5 13.5 %all-to-all-start.2 = ((bf16[4,1,16,16,256]{4,3,2,1,0:T(8,128)(2,1)}), bf16[4,1,16,16,256]{4,3,2,1,0:T(8,128)(2,1)S(1)}, u32[]{:S(2)}, u32[]{:S(2)}) async-start(bf16[4,1,16,16,256]{4,3,2,1,0:T(8,128)(2,1)} %pad_maximum_fusion.1), calls=%async_computation.2 | async-start | bytes 1048576 | tf_op jit(solution)/shard_map/all_to_all | solution.py:175
  71.0 13.1 %all-to-all-start.3 = ((bf16[4,1,16,16,256]{4,3,2,1,0:T(8,128)(2,1)}), bf16[4,1,16,16,256]{4,3,2,1,0:T(8,128)(2,1)}, u32[]{:S(2)}, u32[]{:S(2)}) async-start(bf16[4,1,16,16,256]{4,3,2,1,0:T(8,128)(2,1)} %pad_maximum_fusion.2), calls=%async_computation.3 | async-start | bytes 1048576 | tf_op jit(solution)/shard_map/all_to_all | solution.py:175
  87.1 3.8 %copy-start.7 = (bf16[2048,256]{1,0:T(8,128)(2,1)}, bf16[2048,256]{1,0:T(8,128)(2,1)S(1)}, u32[]{:S(2)}) copy-start(bf16[2048,256]{1,0:T(8,128)(2,1)S(1)} %add_convert_fusion) | copy-start | bytes 3145732
  87.1 3.8 %copy-start.2 = (bf16[1,16,128,256]{3,2,1,0:T(8,128)(2,1)S(1)}, bf16[1,16,128,256]{3,2,1,0:T(8,128)(2,1)}, u32[]{:S(2)}) copy-start(bf16[1,16,128,256]{3,2,1,0:T(8,128)(2,1)} %param.11) | copy-start | bytes 3145732
  87.2 3.8 %copy-start.4 = (bf16[1,16,128,256]{3,2,1,0:T(8,128)(2,1)S(1)}, bf16[1,16,128,256]{3,2,1,0:T(8,128)(2,1)}, u32[]{:S(2)}) copy-start(bf16[1,16,128,256]{3,2,1,0:T(8,128)(2,1)} %param.12) | copy-start | bytes 3145732
  87.2 3.8 %copy-start.17 = (f32[256]{0:T(256)S(1)}, f32[256]{0:T(256)}, u32[]{:S(2)}) copy-start(f32[256]{0:T(256)} %param.21) | copy-start | bytes 3076
  87.2 3.8 %copy-start.18 = (bf16[1024,256]{1,0:T(8,128)(2,1)S(1)}, bf16[1024,256]{1,0:T(8,128)(2,1)}, u32[]{:S(2)}) copy-start(bf16[1024,256]{1,0:T(8,128)(2,1)} %param.19) | copy-start | bytes 1572868
  87.2 3.8 %copy-start.20 = (f32[256]{0:T(256)S(1)}, f32[256]{0:T(256)}, u32[]{:S(2)}) copy-start(f32[256]{0:T(256)} %param.20) | copy-start | bytes 3076
  106.4 18.8 %all-to-all-start.4 = ((bf16[4,1,16,32,256]{4,3,2,1,0:T(8,128)(2,1)}), bf16[4,1,16,32,256]{4,3,2,1,0:T(8,128)(2,1)}, u32[]{:S(2)}, u32[]{:S(2)}) async-start(bf16[4,1,16,32,256]{4,3,2,1,0:T(8,128)(2,1)} %bitcast.326), calls=%async_computation.4 | async-start | bytes 2097152 | tf_op jit(solution)/shard_map/all_to_all | solution.py:121
  110.7 107.5 %all-reduce.10.cloned.1.call-start = ((), (), s32[]{:S(2)}) async-start(), calls=%async_computation.8 | async-start | bytes 4194304 | tf_op jit(solution)/shard_map/psum | solution.py:222
  115.8 10.9 %copy-start.11 = (f32[1,256]{1,0:T(1,128)S(1)}, f32[1,256]{1,0:T(1,128)}, u32[]{:S(2)}) copy-start(f32[1,256]{1,0:T(1,128)} %get-tuple-element.198) | copy-start | bytes 3076
  115.8 10.9 %copy-start.13 = (f32[1,256]{1,0:T(1,128)S(1)}, f32[1,256]{1,0:T(1,128)}, u32[]{:S(2)}) copy-start(f32[1,256]{1,0:T(1,128)} %get-tuple-element.199) | copy-start | bytes 3076
  126.7 21.6 %copy-start.1 = (f32[4,1,16,32,256]{4,3,2,0,1:T(8,128)}, f32[4,1,16,32,256]{4,3,2,0,1:T(8,128)S(1)}, u32[]{:S(2)}) copy-start(f32[4,1,16,32,256]{4,3,2,0,1:T(8,128)S(1)} %bitcast_convert_fusion) | copy-start | bytes 6291460
  153.1 18.8 %all-to-all-start.5 = ((bf16[1,64,32,256]{3,2,0,1:T(8,128)(2,1)}), bf16[1,64,32,256]{3,2,0,1:T(8,128)(2,1)}, u32[]{:S(2)}, u32[]{:S(2)}) async-start(bf16[1,64,32,256]{3,2,0,1:T(8,128)(2,1)} %fusion.675), calls=%async_computation.5 | async-start | bytes 2097152 | tf_op jit(solution)/shard_map/all_to_all | solution.py:213
  169.0 4.3 %copy-start.3 = (bf16[1,16,128,256]{3,2,1,0:T(8,128)(2,1)S(1)}, bf16[1,16,128,256]{3,2,1,0:T(8,128)(2,1)}, u32[]{:S(2)}) copy-start(bf16[1,16,128,256]{3,2,1,0:T(8,128)(2,1)} %param.11) | copy-start | bytes 3145732
  187.3 7.7 %copy-start.5 = (bf16[1,16,128,256]{3,2,1,0:T(8,128)(2,1)S(1)}, bf16[1,16,128,256]{3,2,1,0:T(8,128)(2,1)}, u32[]{:S(2)}) copy-start(bf16[1,16,128,256]{3,2,1,0:T(8,128)(2,1)} %param.12) | copy-start | bytes 3145732
  188.4 23.1 %all-to-all-start.6 = ((f32[16,14,128]{2,1,0:T(8,128)}), f32[16,14,128]{2,1,0:T(8,128)S(1)}, u32[]{:S(2)}, u32[]{:S(2)}) async-start(f32[16,14,128]{2,1,0:T(8,128)} %reshape.810), calls=%async_computation.6 | async-start | bytes 262144 | tf_op jit(solution)/shard_map/all_to_all | solution.py:258
  212.2 13.4 %all-to-all-start.7 = ((f32[16,14,128]{2,1,0:T(8,128)}), f32[16,14,128]{2,1,0:T(8,128)S(1)}, u32[]{:S(2)}, u32[]{:S(2)}) async-start(f32[16,14,128]{2,1,0:T(8,128)} %broadcast_in_dim.8), calls=%async_computation.7 | async-start | bytes 262144 | tf_op jit(solution)/shard_map/all_to_all | solution.py:261
  218.2 11.5 %copy-start.8 = (f32[256,1024]{1,0:T(8,128)S(1)}, f32[256,1024]{1,0:T(8,128)}, u32[]{:S(2)}) copy-start(f32[256,1024]{1,0:T(8,128)} %get-tuple-element.274) | copy-start | bytes 3145732
  (7 other events, 9.5 us)
Sparse Core Ops, SparseCore 0:
  115.9 101.9 all-reduce.9
